TPU v7x, 32 devices: a whole 2x2x4 slice. The times are simulated.
32 devices in a mesh: expert: 8 (over z, x), tensor: 4 (over y, core).
Axes of the slice: x: 2, y: 2, z: 4, core: 2. Of those that a mesh axis runs over, the one named last changes fastest.
Arguments:
- context: bfloat16 [2048, 2048], P('expert', 'tensor'), may hold values from -0.25976562 to 0.25976562
- out_proj: bfloat16 [2048, 2048], P('tensor'), may hold values from -0.125 to 0.125
- residual: bfloat16 [2048, 2048], P(('expert', 'tensor')), may hold values from -0.25976562 to 0.25976562
- norm_gain: float32 [2048], replicated, may hold values from 0.1 to 1.9
- router_weight: float32 [2048, 64], replicated, may hold values from -5.524272 to 5.524272
- expert_ids: int32 [2048, 8], P('expert'), may hold values from 0 to 63, all different within a row; in each aligned block of 64 rows (0 to 63, 64 to 127, ...) at most 10 rows name the same one
- placement: int32 [128], replicated, may hold values from 0 to 63, as said below
- expert_weights: bfloat16 [128, 3, 2048, 1024], P('expert', None, None, 'tensor'), as said below
- post_gain: float32 [2048], replicated, may hold values from 0.5 to 1.5
Outputs:
- hidden_out: float32 [2048, 2048], P(('expert', 'tensor'))
- normed_out: float32 [2048, 2048], P(('expert', 'tensor'))
Inputs may be any that keep to these rules, and one draw needn't show every extreme that they name: `expert_ids`: each row names 8 different experts. In each aligned block of 64 rows (the rows of one device) no expert is named by more than 10 rows, a bound that some block reaches; every expert is named somewhere. `placement`: every expert is held by one, three or five slots. `expert_weights`: slots that hold the same expert carry equal weights.
All inputs are finite; a program needn't handle non-finite values.
Results may differ from a plain program's by a relative error of at most 0.018.
Values may be sent and summed in bfloat16 or wider, within the bound.
No kernel may reach another device: no remote copies, remote signals or barrier semaphores. Data moves between devices by JAX's collectives and lax.ppermute only.
A program may use at most 256 MiB of HBM per device.

v0:
```python
import jax
import jax.numpy as jnp
from jax import lax
from jax.sharding import PartitionSpec as P

EPS = 1e-06


def rms_scale(values, gain_row):
    mean_square = jnp.mean(values * values, axis=-1, keepdims=True)
    return values * lax.rsqrt(mean_square + EPS) * gain_row


def expert_partial(block_rows, weights):
    gate_pre = jnp.einsum(
        "nqsmd,sdf->nqsmf", block_rows, weights[:, 0], preferred_element_type=jnp.float32
    )
    up_pre = jnp.einsum(
        "nqsmd,sdf->nqsmf", block_rows, weights[:, 1], preferred_element_type=jnp.float32
    )
    inner_act = (jax.nn.silu(gate_pre) * up_pre).astype(jnp.bfloat16)
    return jnp.einsum(
        "nqsmf,sdf->nqsmd", inner_act, weights[:, 2], preferred_element_type=jnp.float32
    )


def on_device(
    context,
    out_proj,
    residual,
    norm_gain,
    router_weight,
    expert_ids,
    placement,
    expert_weights,
    post_gain,
):
    groups = lax.axis_size("tensor")
    holders = lax.axis_size("expert")
    my_group = lax.axis_index("tensor")
    my_holder = lax.axis_index("expert")
    row_count = residual.shape[0]
    model_width = residual.shape[1]
    top_count = expert_ids.shape[1]
    expert_count = router_weight.shape[1]
    slot_dev = expert_weights.shape[0]
    slot_total = placement.shape[0]
    blocks = holders * groups
    capacity = max(2, row_count * top_count * 5 // (expert_count * 4))
    expert_range = jnp.arange(expert_count, dtype=jnp.int32)
    slot_range = jnp.arange(slot_total, dtype=jnp.int32)
    attention = lax.psum_scatter(
        jnp.dot(context, out_proj, preferred_element_type=jnp.float32).astype(jnp.bfloat16),
        "tensor",
        scatter_dimension=0,
        tiled=True,
    ).astype(jnp.float32)
    hidden_mid = residual.astype(jnp.float32) + attention
    normed_full = rms_scale(hidden_mid, norm_gain)
    normed = normed_full.astype(jnp.bfloat16)
    logits = jnp.dot(normed_full, router_weight, precision=lax.Precision.HIGHEST)
    own_ids = lax.dynamic_slice_in_dim(expert_ids, my_group * row_count, row_count, 0)
    own_onehot = own_ids[:, :, None] == expert_range[None, None, :]
    chosen = jnp.sum(jnp.where(own_onehot, logits[:, None, :], 0.0), axis=-1)
    gate_weights = jax.nn.softmax(chosen, axis=-1)
    all_rows = lax.all_gather(normed, ("expert", "tensor"), axis=0, tiled=True)
    all_ids = lax.all_gather(expert_ids, "expert", axis=0, tiled=True)
    holds = (placement[None, :] == expert_range[:, None]).astype(jnp.int32)
    copies = jnp.sum(holds, axis=1)
    copy_rank = jnp.cumsum(holds, axis=1) - 1
    holder_range = jnp.arange(holders, dtype=jnp.int32)
    copy_pick = holder_range[:, None] % copies[None, :]
    picked = (holds[None] > 0) & (copy_rank[None] == copy_pick[:, :, None])
    slot_pick = jnp.sum(jnp.where(picked, slot_range[None, None, :], 0), axis=2)
    flat_ids = all_ids.reshape(blocks, row_count * top_count)
    block_holder = jnp.arange(blocks, dtype=jnp.int32) // groups
    block_pick = slot_pick[block_holder]
    onehot = flat_ids[:, :, None] == expert_range
    slot_of = jnp.sum(jnp.where(onehot, block_pick[:, None, :], 0), axis=-1)
    slot_hot = (slot_of[:, :, None] == slot_range).astype(jnp.int32)
    rank_all = jnp.sum(jnp.cumsum(slot_hot, axis=1) * slot_hot, axis=-1) - 1
    holder_all = slot_of // slot_dev
    local_all = slot_of % slot_dev
    block_ids = jnp.arange(blocks, dtype=jnp.int32)[:, None]
    token_of = (
        block_ids * row_count
        + jnp.arange(row_count * top_count, dtype=jnp.int32)[None, :] // top_count
    )
    mine = holder_all == my_holder
    row_total = blocks * slot_dev * capacity
    target = jnp.where(mine, (block_ids * slot_dev + local_all) * capacity + rank_all, row_total)
    index_table = (
        jnp.zeros((row_total,), jnp.int32)
        .at[target.reshape(-1)]
        .set(token_of.reshape(-1), mode="drop", unique_indices=True)
    )
    received = jnp.take(all_rows, index_table, axis=0).reshape(
        holders, groups, slot_dev, capacity, model_width
    )
    own_block = my_holder * groups + my_group
    holder = lax.dynamic_index_in_dim(holder_all, own_block, 0, keepdims=False)
    local_slot = lax.dynamic_index_in_dim(local_all, own_block, 0, keepdims=False)
    rank_in = lax.dynamic_index_in_dim(rank_all, own_block, 0, keepdims=False)
    partial_value = expert_partial(received, expert_weights)
    expert_sum = lax.psum_scatter(
        partial_value.astype(jnp.bfloat16), "tensor", scatter_dimension=1, tiled=True
    )
    returned = lax.all_to_all(expert_sum, "expert", split_axis=0, concat_axis=0, tiled=True)
    own_index = (holder * slot_dev + local_slot) * capacity + rank_in
    outputs = returned.reshape(-1, model_width)[own_index].reshape(
        row_count, top_count, model_width
    )
    moe_sum = jnp.einsum("rk,rkd->rd", gate_weights, outputs.astype(jnp.float32))
    hidden_out = hidden_mid + moe_sum
    normed_out = rms_scale(hidden_out, post_gain)
    return (hidden_out, normed_out)


def solution(mesh):
    in_specs = (
        P("expert", "tensor"),
        P("tensor", None),
        P(("expert", "tensor"), None),
        P(),
        P(),
        P("expert", None),
        P(),
        P("expert", None, None, "tensor"),
        P(),
    )
    out_specs = (P(("expert", "tensor"), None), P(("expert", "tensor"), None))
    return jax.shard_map(
        on_device, mesh=mesh, in_specs=in_specs, out_specs=out_specs, check_vma=False
    )
```

profile of v0, /device:TPU:0, one launch (start us, length us, event | category | flops | bytes accessed | tf_op | source)
XLA Modules:
  0.0 628.9 jit_solution(16265701694805310592)
XLA Ops:
  7.2 1.5 copy-done
  8.8 2.7 convolution_convert_fusion
  11.5 27.7 %reduce-scatter.3.cloned.1.call-done = bf16[64,2048]{1,0:T(8,128)(2,1)} async-done(((bf16[256,2048]{1,0:T(8,128)(2,1)}), bf16[64,2048]{1,0:T(8,128)(2,1)}) %reduce-scatter.3.cloned.1.call-update) | async-done | bytes 262160 | tf_op jit(solution)/shard_map/reduce_scatter | solution.py:52
  39.2 1.2 multiply_reduce_fusion.1
  40.4 1.8 fusion.29
  42.6 30.9 %all_gather.6 = s32[2048,8]{0,1:T(8,128)S(1)} all-gather(s32[256,8]{0,1:T(8,128)} %param.14), channel_id=1, replica_groups=mesh['expert'=8,'tensor'=4] {'expert'}, dimensions={0}, use_global_device_ids=true | all-gather | bytes 73728 | tf_op jit(solution)/shard_map/all_gather | solution.py:67
  73.5 0.3 copy.65
  73.8 0.5 eq.116
  75.0 0.3 select_reduce_fusion.2
  75.3 0.6 gather_fusion
  75.9 0.8 select_reduce_fusion.1
  76.9 2.5 fusion.14
  79.4 1.1 broadcast_add_fusion
  80.5 11.7 %select_reduce_fusion = s32[32,512]{0,1:T(8,128)S(1)} fusion(s32[32,512,128]{2,0,1:T(8,128)S(1)} %bitcast.112, s32[32,512]{0,1:T(8,128)S(1)} %copy.66), kind=kLoop, calls=%fused_computation.23 | loop fusion | flops 6275072 | bytes 8519680 | tf_op jit(solution)/shard_map/reduce_sum | solution.py:81
  92.3 0.7 broadcast_add_fusion.1
  93.0 0.6 compare_select_fusion
  93.6 60.5 %scatter_custom_fusion = s32[5120]{0:T(1024)S(1)} fusion(s32[16384]{0:T(1024)S(1)} %bitcast.120, s32[16384]{0:T(1024)S(1)} %bitcast.119, s32[]{:T(128)} %constant.121.clone.1), kind=kCustom, calls=%fused_computation.75 | custom fusion | bytes 20484 | tf_op jit(solution)/shard_map/scatter | solution.py:95
  154.5 43.3 %gather_fusion.1 = bf16[5120,2048]{1,0:T(8,128)(2,1)} fusion(bf16[2048,2048]{1,0:T(8,128)(2,1)} %all-gather.2.cloned.1.call-done, s32[5120]{0:T(1024)S(1)} %fusion.38), kind=kCustom, calls=%fused_computation.1 | custom fusion | bytes 41963520 | tf_op jit(solution)/shard_map/jit(_take)/gather | solution.py:97
  197.8 34.0 %gather.14 = bf16[8,4,16,10,2048]{4,3,2,1,0:T(8,128)(2,1)} reshape(bf16[5120,2048]{1,0:T(8,128)(2,1)} %gather_fusion.1) | data formatting | bytes 41943040 | tf_op jit(solution)/shard_map/jit(_take)/gather | solution.py:97
  231.8 20.7 %fusion = f32[16,8,4,10,256]{4,3,2,1,0:T(8,128)} fusion(bf16[16,3,2048,256]{3,2,1,0:T(8,128)(2,1)} %param.16, bf16[8,4,16,10,2048]{4,3,2,1,0:T(8,128)(2,1)} %gather.14, pred[8,4,16,10]{3,2,1,0:T(8,128)(4,1)S(1)} %broadcast_in_dim.96), kind=kOutput, calls=%fused_computation.6 | convolution fusion | flops 5379194880 | bytes 55579648 | tf_op jit(solution)/shard_map/nqsmd,sdf->nqsmf/dot_general | solution.py:18
  252.5 39.2 %convert_bitcast_fusion = bf16[8,4,16,10,2048]{4,3,1,0,2:T(8,128)(2,1)} fusion(bf16[16,3,2048,256]{3,2,1,0:T(8,128)(2,1)} %param.16, f32[16,8,4,10,256]{4,3,2,1,0:T(8,128)} %fusion, bf16[8,4,16,10,2048]{4,3,2,1,0:T(8,128)(2,1)} %gather.14, pred[8,4,16,10]{3,2,1,0:T(8,128)(4,1)S(1)} %broadcast_in_dim.96), kind=kOutput, calls=%fused_computation.4 | convolution fusion | flops 10766254080 | bytes 96474112 | tf_op jit(solution)/shard_map/nqsmf,sdf->nqsmd/dot_general | solution.py:22
  291.7 24.3 %copy.74 = bf16[8,4,16,10,2048]{4,2,3,0,1:T(8,128)(2,1)} copy(bf16[8,4,16,10,2048]{4,3,1,0,2:T(8,128)(2,1)} %convert_bitcast_fusion) | data formatting | bytes 41943040 | tf_op jit(solution)/shard_map/convert_element_type | solution.py:106
  316.1 153.2 %reduce-scatter.5.cloned.1.call-done = bf16[8,1,16,10,2048]{4,2,3,0,1:T(8,128)(2,1)} async-done(((bf16[8,4,16,10,2048]{4,2,3,0,1:T(8,128)(2,1)}), bf16[8,1,16,10,2048]{4,2,3,0,1:T(8,128)(2,1)}) %reduce-scatter.5.cloned.1.call-update) | async-done | bytes 5242896 | tf_op jit(solution)/shard_map/reduce_scatter | solution.py:105
  469.3 5.5 all-to-all-start
  475.1 0.8 compare_select_fusion.6
  475.9 0.7 fusion.30
  477.1 113.5 %all-to-all-done = bf16[8,1,16,10,2048]{4,2,3,1,0:T(8,128)(2,1)} async-done(((bf16[8,1,16,10,2048]{4,2,3,1,0:T(8,128)(2,1)}), bf16[8,1,16,10,2048]{4,2,3,1,0:T(8,128)(2,1)}, u32[]{:S(2)}, u32[]{:S(2)}) %all-to-all-start) | async-done | bytes 5242912 | tf_op jit(solution)/shard_map/all_to_all | solution.py:108
  590.6 9.7 %copy.76 = bf16[8,1,16,10,2048]{4,3,2,0,1:T(8,128)(2,1)} copy(bf16[8,1,16,10,2048]{4,2,3,1,0:T(8,128)(2,1)} %all-to-all-done) | data formatting | bytes 10485760 | tf_op jit(solution)/shard_map/all_to_all | solution.py:108
  600.3 10.0 %reshape.449 = bf16[1280,2048]{1,0:T(8,128)(2,1)} reshape(bf16[8,1,16,10,2048]{4,3,2,0,1:T(8,128)(2,1)} %copy.76) | data formatting | bytes 10485760 | tf_op jit(solution)/shard_map/reshape | solution.py:110
  610.3 8.5 %gather_fusion.2 = bf16[512,2048]{1,0:T(8,128)(2,1)} fusion(bf16[1280,2048]{1,0:T(8,128)(2,1)} %reshape.449, s32[1024]{0:T(1024)S(1)} %pad_clamp_fusion), kind=kCustom, calls=%fused_computation.2 | custom fusion | bytes 4196352 | tf_op jit(solution)/shard_map/gather | solution.py:110
  618.8 2.3 fusion.27
  621.4 0.9 multiply_multiply_fusion
  (72 shorter events, 2.8 us)
Async XLA Ops:
  7.2 1.6 copy-start
  7.2 67.2 %copy-start.13 = (s32[128]{0:T(128)S(1)}, s32[128]{0:T(128)}, u32[]{:S(2)}) copy-start(s32[128]{0:T(128)} %param.15) | copy-start | bytes 1540
  7.2 32.0 %reduce-scatter.3.cloned.1.call-start = ((), (), s32[]{:S(2)}) async-start(), calls=%async_computation.3 | async-start | bytes 1310720 | tf_op jit(solution)/shard_map/reduce_scatter | solution.py:52
  11.4 143.0 %all-gather.2.cloned.1.call-start = ((), (), s32[]{:S(2)}) async-start(), calls=%async_computation.4 | async-start | bytes 8650752 | tf_op jit(solution)/shard_map/all_gather | solution.py:66
  40.4 2.0 copy-start.11
  42.3 427.0 %reduce-scatter.5.cloned.1.call-start = ((), (), s32[]{:S(2)}) async-start(), calls=%async_computation.5 | async-start | bytes 26214400 | tf_op jit(solution)/shard_map/reduce_scatter | solution.py:105
  76.7 3.8 copy-start.5
  316.0 158.8 %copy-start.9 = (s32[256,8]{0,1:T(8,128)S(1)}, s32[256,8]{0,1:T(8,128)}, u32[]{:S(2)}) copy-start(s32[256,8]{0,1:T(8,128)} %param.14) | copy-start | bytes 24580
  316.0 159.0 %copy-start.6 = (s32[32,512]{1,0:T(8,128)S(1)}, s32[32,512]{1,0:T(8,128)}, u32[]{:S(2)}) copy-start(s32[32,512]{1,0:T(8,128)} %copy-done.5) | copy-start | bytes 196612
  316.1 159.8 %copy-start.2 = (bf16[64,2048]{1,0:T(8,128)(2,1)S(1)}, bf16[64,2048]{1,0:T(8,128)(2,1)}, u32[]{:S(2)}) copy-start(bf16[64,2048]{1,0:T(8,128)(2,1)} %param.11) | copy-start | bytes 786436
  316.1 159.8 %copy-start.3 = (bf16[64,2048]{1,0:T(8,128)(2,1)S(1)}, bf16[64,2048]{1,0:T(8,128)(2,1)}, u32[]{:S(2)}) copy-start(bf16[64,2048]{1,0:T(8,128)(2,1)} %reduce-scatter.3.cloned.1.call-done) | copy-start | bytes 786436
  316.1 159.8 %copy-start.7 = (f32[2048,64]{0,1:T(8,128)S(1)}, f32[2048,64]{0,1:T(8,128)}, u32[]{:S(2)}) copy-start(f32[2048,64]{0,1:T(8,128)} %param.13) | copy-start | bytes 1572868
  316.1 159.8 %copy-start.8 = (f32[2048]{0:T(1024)S(1)}, f32[2048]{0:T(1024)}, u32[]{:S(2)}) copy-start(f32[2048]{0:T(1024)} %param.12) | copy-start | bytes 24580
  316.1 159.8 %copy-start.12 = (f32[64]{0:T(128)S(1)}, f32[64]{0:T(128)}, u32[]{:S(2)}) copy-start(f32[64]{0:T(128)} %copy-done.11) | copy-start | bytes 772
  469.3 121.3 %all-to-all-start = ((bf16[8,1,16,10,2048]{4,2,3,1,0:T(8,128)(2,1)}), bf16[8,1,16,10,2048]{4,2,3,1,0:T(8,128)(2,1)}, u32[]{:S(2)}, u32[]{:S(2)}) async-start(bf16[8,1,16,10,2048]{4,2,3,1,0:T(8,128)(2,1)} %bitcast.113), calls=%async_computation.2 | async-start | bytes 10485760 | tf_op jit(solution)/shard_map/all_to_all | solution.py:108
  600.3 22.0 %copy-start.1 = (bf16[512,2048]{1,0:T(8,128)(2,1)S(1)}, bf16[512,2048]{1,0:T(8,128)(2,1)}, u32[]{:S(2)}) copy-start(bf16[512,2048]{1,0:T(8,128)(2,1)} %param.10) | copy-start | bytes 6291460
  610.3 11.1 %copy-start.10 = (f32[2048]{0:T(1024)S(1)}, f32[2048]{0:T(1024)}, u32[]{:S(2)}) copy-start(f32[2048]{0:T(1024)} %param.17) | copy-start | bytes 24580
  621.4 1.0 copy-start.4
Sparse Core Ops, SparseCore 0:
  11.6 27.5 reduce-scatter.2
  43.0 77.6 all-gather.1
  316.2 153.1 reduce-scatter.4
where the time goes:
time: 631 us; the launch traced here: 629 us
  waiting for transfers between devices  294 us (47%)
  local copies, waits for them, and re-layouts  194 us (31%)
  matrix products  65.5 us (10%)
  blocking collectives  30.9 us (5%)
  other arithmetic  23.8 us (4%)
  between operations  14.2 us (2%)
    reduce_scatter x1, waiting for transfers between devices, on_device(): lax.psum_scatter(partial_value.astype(jnp.bfloat16), 'tensor', scatter_di...  153 us
    all_to_all x1, waiting for transfers between devices, on_device(): lax.all_to_all(expert_sum, 'expert', split_axis=0, concat_axis=0, tiled=T...  113 us
    gather x2, local copies, waits for them, and re-layouts, on_device(): jnp.take(all_rows, index_table, axis=0)  77.3 us
    scatter x1, local copies, waits for them, and re-layouts, on_device(): index_table = jnp.zeros((row_total,), jnp.int32).at[target.reshape(-1)].s...  60.5 us
    dot_general x1, matrix products, expert_partial(): jnp.einsum('nqsmf,sdf->nqsmd', inner_act, weights[:, 2], preferred_elemen...  39.2 us
    all_gather x1, blocking collectives, on_device(): all_ids = lax.all_gather(expert_ids, 'expert', axis=0, tiled=True)  30.9 us
    reduce_scatter x1, waiting for transfers between devices, on_device(): lax.psum_scatter(jnp.dot(context, out_proj, preferred_element_type=jnp.fl...  27.7 us
    convert_element_type x1, local copies, waits for them, and re-layouts, on_device(): partial_value.astype(jnp.bfloat16)  24.3 us
  transfers between devices with their start and end apart: 4, of which 3 were waited for; matrix products, arithmetic and copies ran while one was open for 13% of the time, Pallas kernels for 0%

commit v1 on v0

--- a/solution.py
+++ b/solution.py
@@ -64,7 +64,14 @@
     chosen = jnp.sum(jnp.where(own_onehot, logits[:, None, :], 0.0), axis=-1)
     gate_weights = jax.nn.softmax(chosen, axis=-1)
     all_rows = lax.all_gather(normed, ("expert", "tensor"), axis=0, tiled=True)
-    all_ids = lax.all_gather(expert_ids, "expert", axis=0, tiled=True)
+    ring = [expert_ids]
+    for hop in range(7):
+        ring.append(lax.ppermute(ring[-1], "expert", [(dev, (dev + 1) % 8) for dev in range(8)]))
+    all_ids = jnp.roll(
+        jnp.concatenate(ring[::-1], axis=0),
+        (lax.axis_index("expert") + 1) * ring[0].shape[0],
+        axis=0,
+    )
     holds = (placement[None, :] == expert_range[:, None]).astype(jnp.int32)
     copies = jnp.sum(holds, axis=1)
     copy_rank = jnp.cumsum(holds, axis=1) - 1

time: 631 us -> 641 us (1.016)
  waiting for transfers between devices: 294 us -> 331 us
  blocking collectives: 30.9 us -> 0 us
    ppermute x0 -> x7, waiting for transfers between devices: none -> 40.4 us  [on_device(): lax.ppermute(ring[-1], 'expert', [(dev, (dev + 1) % 8) for dev in range(8)])]
    all_gather x1 -> x0, blocking collectives: 30.9 us -> none  [on_device(): all_ids = lax.all_gather(expert_ids, 'expert', axis=0, tiled=True)]
  transfers between devices with their start and end apart: 4 -> 11, of which waited for: 3 -> 10; matrix products, arithmetic and copies ran while one was open for 13% -> 13% of each run, Pallas kernels for 0% -> 0%
where the time goes in v1:
time: 641 us; the launch traced here: 639 us
  waiting for transfers between devices  331 us (52%)
  local copies, waits for them, and re-layouts  196 us (31%)
  matrix products  65.5 us (10%)
  other arithmetic  25.1 us (4%)
  between operations  14.2 us (2%)
  starting transfers between devices  7.18 us (1%)
    reduce_scatter x1, waiting for transfers between devices, on_device(): lax.psum_scatter(partial_value.astype(jnp.bfloat16), 'tensor', scatter_di...  150 us
    all_to_all x1, waiting for transfers between devices, on_device(): lax.all_to_all(expert_sum, 'expert', split_axis=0, concat_axis=0, tiled=T...  113 us
    gather x2, local copies, waits for them, and re-layouts, on_device(): jnp.take(all_rows, index_table, axis=0)  77.3 us
    scatter x1, local copies, waits for them, and re-layouts, on_device(): index_table = jnp.zeros((row_total,), jnp.int32).at[target.reshape(-1)].s...  60.5 us
    ppermute x7, waiting for transfers between devices, on_device(): lax.ppermute(ring[-1], 'expert', [(dev, (dev + 1) % 8) for dev in range(8)])  40.4 us
    dot_general x1, matrix products, expert_partial(): jnp.einsum('nqsmf,sdf->nqsmd', inner_act, weights[:, 2], preferred_elemen...  39.2 us
    reduce_scatter x1, waiting for transfers between devices, on_device(): lax.psum_scatter(jnp.dot(context, out_proj, preferred_element_type=jnp.fl...  27.7 us
    convert_element_type x1, local copies, waits for them, and re-layouts, on_device(): partial_value.astype(jnp.bfloat16)  24.3 us
  transfers between devices with their start and end apart: 11, of which 10 were waited for; matrix products, arithmetic and copies ran while one was open for 13% of the time, Pallas kernels for 0%

profile of v1, /device:TPU:0, one launch (start us, length us, event | category | flops | bytes accessed | tf_op | source)
XLA Modules:
  0.0 639.0 jit_solution(3062658876069556056)
XLA Ops:
  7.2 1.5 copy-done
  8.8 2.7 convolution_convert_fusion
  11.5 27.7 %reduce-scatter.3.cloned.1.call-done = bf16[64,2048]{1,0:T(8,128)(2,1)} async-done(((bf16[256,2048]{1,0:T(8,128)(2,1)}), bf16[64,2048]{1,0:T(8,128)(2,1)}) %reduce-scatter.3.cloned.1.call-update) | async-done | bytes 262160 | tf_op jit(solution)/shard_map/reduce_scatter | solution.py:52
  39.2 1.2 multiply_reduce_fusion.1
  40.4 1.8 fusion.29
  42.3 1.5 collective-permute-start
  45.0 0.8 fusion.36
  45.8 3.2 collective-permute-done
  49.0 6.4 %collective-permute-done.1 = s32[256,8]{0,1:T(8,128)S(1)} collective-permute-done((s32[256,8]{0,1:T(8,128)S(1)}, s32[256,8]{0,1:T(8,128)S(1)}, u32[]{:S(2)}, u32[]{:S(2)}) %collective-permute-start.1) | collective-permute-done | bytes 8224 | tf_op jit(solution)/shard_map/ppermute | solution.py:69
  55.4 6.4 collective-permute-done.2
  61.9 6.2 collective-permute-done.3
  68.5 6.1 collective-permute-done.4
  74.6 6.3 collective-permute-done.5
  81.7 5.7 collective-permute-done.6
  89.7 0.8 select_reduce_fusion.1
  90.8 2.5 fusion.14
  93.3 1.1 broadcast_add_fusion
  94.4 11.7 %select_reduce_fusion = s32[32,512]{0,1:T(8,128)S(1)} fusion(s32[32,512,128]{2,0,1:T(8,128)S(1)} %bitcast.112, s32[32,512]{0,1:T(8,128)S(1)} %copy.66), kind=kLoop, calls=%fused_computation.23 | loop fusion | flops 6275072 | bytes 8519680 | tf_op jit(solution)/shard_map/reduce_sum | solution.py:88
  107.5 60.5 %scatter_custom_fusion = s32[5120]{0:T(1024)S(1)} fusion(s32[16384]{0:T(1024)S(1)} %bitcast.120, s32[16384]{0:T(1024)S(1)} %bitcast.119, s32[]{:T(128)} %constant.140.clone.1), kind=kCustom, calls=%fused_computation.91 | custom fusion | bytes 20484 | tf_op jit(solution)/shard_map/scatter | solution.py:102
  168.4 43.3 %gather_fusion.1 = bf16[5120,2048]{1,0:T(8,128)(2,1)} fusion(bf16[2048,2048]{1,0:T(8,128)(2,1)} %all-gather.2.cloned.1.call-done, s32[5120]{0:T(1024)S(1)} %fusion.38), kind=kCustom, calls=%fused_computation.1 | custom fusion | bytes 41963520 | tf_op jit(solution)/shard_map/jit(_take)/gather | solution.py:104
  211.7 34.0 %gather.14 = bf16[8,4,16,10,2048]{4,3,2,1,0:T(8,128)(2,1)} reshape(bf16[5120,2048]{1,0:T(8,128)(2,1)} %gather_fusion.1) | data formatting | bytes 41943040 | tf_op jit(solution)/shard_map/jit(_take)/gather | solution.py:104
  245.7 20.7 %fusion = f32[16,8,4,10,256]{4,3,2,1,0:T(8,128)} fusion(bf16[16,3,2048,256]{3,2,1,0:T(8,128)(2,1)} %param.16, bf16[8,4,16,10,2048]{4,3,2,1,0:T(8,128)(2,1)} %gather.14, pred[8,4,16,10]{3,2,1,0:T(8,128)(4,1)S(1)} %broadcast_in_dim.96), kind=kOutput, calls=%fused_computation.6 | convolution fusion | flops 5379194880 | bytes 55579648 | tf_op jit(solution)/shard_map/nqsmd,sdf->nqsmf/dot_general | solution.py:18
  266.4 39.2 %convert_bitcast_fusion = bf16[8,4,16,10,2048]{4,3,1,0,2:T(8,128)(2,1)} fusion(bf16[16,3,2048,256]{3,2,1,0:T(8,128)(2,1)} %param.16, f32[16,8,4,10,256]{4,3,2,1,0:T(8,128)} %fusion, bf16[8,4,16,10,2048]{4,3,2,1,0:T(8,128)(2,1)} %gather.14, pred[8,4,16,10]{3,2,1,0:T(8,128)(4,1)S(1)} %broadcast_in_dim.96), kind=kOutput, calls=%fused_computation.4 | convolution fusion | flops 10766254080 | bytes 96474112 | tf_op jit(solution)/shard_map/nqsmf,sdf->nqsmd/dot_general | solution.py:22
  305.6 24.3 %copy.74 = bf16[8,4,16,10,2048]{4,2,3,0,1:T(8,128)(2,1)} copy(bf16[8,4,16,10,2048]{4,3,1,0,2:T(8,128)(2,1)} %convert_bitcast_fusion) | data formatting | bytes 41943040 | tf_op jit(solution)/shard_map/convert_element_type | solution.py:113
  330.0 149.5 %reduce-scatter.5.cloned.1.call-done = bf16[8,1,16,10,2048]{4,2,3,0,1:T(8,128)(2,1)} async-done(((bf16[8,4,16,10,2048]{4,2,3,0,1:T(8,128)(2,1)}), bf16[8,1,16,10,2048]{4,2,3,0,1:T(8,128)(2,1)}) %reduce-scatter.5.cloned.1.call-update) | async-done | bytes 5242896 | tf_op jit(solution)/shard_map/reduce_scatter | solution.py:112
  479.5 5.5 all-to-all-start
  487.3 113.5 %all-to-all-done = bf16[8,1,16,10,2048]{4,2,3,1,0:T(8,128)(2,1)} async-done(((bf16[8,1,16,10,2048]{4,2,3,1,0:T(8,128)(2,1)}), bf16[8,1,16,10,2048]{4,2,3,1,0:T(8,128)(2,1)}, u32[]{:S(2)}, u32[]{:S(2)}) %all-to-all-start) | async-done | bytes 5242912 | tf_op jit(solution)/shard_map/all_to_all | solution.py:115
  600.7 9.7 %copy.76 = bf16[8,1,16,10,2048]{4,3,2,0,1:T(8,128)(2,1)} copy(bf16[8,1,16,10,2048]{4,2,3,1,0:T(8,128)(2,1)} %all-to-all-done) | data formatting | bytes 10485760 | tf_op jit(solution)/shard_map/all_to_all | solution.py:115
  610.5 10.0 %reshape.449 = bf16[1280,2048]{1,0:T(8,128)(2,1)} reshape(bf16[8,1,16,10,2048]{4,3,2,0,1:T(8,128)(2,1)} %copy.76) | data formatting | bytes 10485760 | tf_op jit(solution)/shard_map/reshape | solution.py:117
  620.5 8.5 %gather_fusion.2 = bf16[512,2048]{1,0:T(8,128)(2,1)} fusion(bf16[1280,2048]{1,0:T(8,128)(2,1)} %reshape.449, s32[1024]{0:T(1024)S(1)} %pad_clamp_fusion), kind=kCustom, calls=%fused_computation.2 | custom fusion | bytes 4196352 | tf_op jit(solution)/shard_map/gather | solution.py:117
  628.9 2.3 fusion.27
  631.6 0.9 multiply_multiply_fusion
  (100 shorter events, 9.2 us)
Async XLA Ops:
  7.2 1.6 copy-start
  7.2 32.0 %reduce-scatter.3.cloned.1.call-start = ((), (), s32[]{:S(2)}) async-start(), calls=%async_computation.3 | async-start | bytes 1310720 | tf_op jit(solution)/shard_map/reduce_scatter | solution.py:52
  11.4 156.9 %all-gather.2.cloned.1.call-start = ((), (), s32[]{:S(2)}) async-start(), calls=%async_computation.4 | async-start | bytes 8650752 | tf_op jit(solution)/shard_map/all_gather | solution.py:66
  40.4 4.1 copy-start.11
  42.3 437.2 %reduce-scatter.5.cloned.1.call-start = ((), (), s32[]{:S(2)}) async-start(), calls=%async_computation.5 | async-start | bytes 26214400 | tf_op jit(solution)/shard_map/reduce_scatter | solution.py:112
  42.3 6.6 %collective-permute-start = (s32[256,8]{0,1:T(8,128)}, s32[256,8]{0,1:T(8,128)S(1)}, u32[]{:S(2)}, u32[]{:S(2)}) collective-permute-start(s32[256,8]{0,1:T(8,128)} %param.14), channel_id=1, source_target_pairs={{0,4},{4,8},{8,12},{12,16},{16,20},{20,24},{24,28},{28,0},{1,5},{5... | collective-permute-start | bytes 24584 | tf_op jit(solution)/shard_map/ppermute | solution.py:69
  49.0 6.5 %collective-permute-start.1 = (s32[256,8]{0,1:T(8,128)S(1)}, s32[256,8]{0,1:T(8,128)S(1)}, u32[]{:S(2)}, u32[]{:S(2)}) collective-permute-start(s32[256,8]{0,1:T(8,128)S(1)} %collective-permute-done), channel_id=1, source_target_pairs={{0,4},{4,8},{8,12},{12,16},{16,20},{20,24},{24,28},{28,0},{1,5},{5... | collective-permute-start | bytes 24584 | tf_op jit(solution)/shard_map/ppermute | solution.py:69
  55.4 6.4 collective-permute-start.2
  61.8 6.3 collective-permute-start.3
  68.1 6.5 %collective-permute-start.4 = (s32[256,8]{0,1:T(8,128)S(1)}, s32[256,8]{0,1:T(8,128)S(1)}, u32[]{:S(2)}, u32[]{:S(2)}) collective-permute-start(s32[256,8]{0,1:T(8,128)S(1)} %collective-permute-done.3), channel_id=1, source_target_pairs={{0,4},{4,8},{8,12},{12,16},{16,20},{20,24},{24,28},{28,0},{1,5},{5... | collective-permute-start | bytes 24584 | tf_op jit(solution)/shard_map/ppermute | solution.py:69
  74.6 6.3 collective-permute-start.5
  81.0 6.4 %collective-permute-start.6 = (s32[256,8]{0,1:T(8,128)S(1)}, s32[256,8]{0,1:T(8,128)S(1)}, u32[]{:S(2)}, u32[]{:S(2)}) collective-permute-start(s32[256,8]{0,1:T(8,128)S(1)} %collective-permute-done.5), channel_id=1, source_target_pairs={{0,4},{4,8},{8,12},{12,16},{16,20},{20,24},{24,28},{28,0},{1,5},{5... | collective-permute-start | bytes 24584 | tf_op jit(solution)/shard_map/ppermute | solution.py:69
  90.6 3.8 copy-start.5
  329.9 155.1 %copy-start.8 = (s32[256,8]{0,1:T(8,128)S(1)}, s32[256,8]{0,1:T(8,128)}, u32[]{:S(2)}) copy-start(s32[256,8]{0,1:T(8,128)} %param.14) | copy-start | bytes 24580
  329.9 155.3 %copy-start.6 = (s32[32,512]{1,0:T(8,128)S(1)}, s32[32,512]{1,0:T(8,128)}, u32[]{:S(2)}) copy-start(s32[32,512]{1,0:T(8,128)} %copy-done.5) | copy-start | bytes 196612
  329.9 156.1 %copy-start.2 = (bf16[64,2048]{1,0:T(8,128)(2,1)S(1)}, bf16[64,2048]{1,0:T(8,128)(2,1)}, u32[]{:S(2)}) copy-start(bf16[64,2048]{1,0:T(8,128)(2,1)} %param.11) | copy-start | bytes 786436
  329.9 156.1 %copy-start.3 = (bf16[64,2048]{1,0:T(8,128)(2,1)S(1)}, bf16[64,2048]{1,0:T(8,128)(2,1)}, u32[]{:S(2)}) copy-start(bf16[64,2048]{1,0:T(8,128)(2,1)} %reduce-scatter.3.cloned.1.call-done) | copy-start | bytes 786436
  330.0 156.1 %copy-start.7 = (f32[2048,64]{0,1:T(8,128)S(1)}, f32[2048,64]{0,1:T(8,128)}, u32[]{:S(2)}) copy-start(f32[2048,64]{0,1:T(8,128)} %param.13) | copy-start | bytes 1572868
  330.0 156.1 %copy-start.9 = (f32[2048]{0:T(1024)S(1)}, f32[2048]{0:T(1024)}, u32[]{:S(2)}) copy-start(f32[2048]{0:T(1024)} %param.12) | copy-start | bytes 24580
  330.0 156.0 %copy-start.12 = (f32[64]{0:T(128)S(1)}, f32[64]{0:T(128)}, u32[]{:S(2)}) copy-start(f32[64]{0:T(128)} %copy-done.11) | copy-start | bytes 772
  479.5 121.2 %all-to-all-start = ((bf16[8,1,16,10,2048]{4,2,3,1,0:T(8,128)(2,1)}), bf16[8,1,16,10,2048]{4,2,3,1,0:T(8,128)(2,1)}, u32[]{:S(2)}, u32[]{:S(2)}) async-start(bf16[8,1,16,10,2048]{4,2,3,1,0:T(8,128)(2,1)} %bitcast.113), calls=%async_computation.2 | async-start | bytes 10485760 | tf_op jit(solution)/shard_map/all_to_all | solution.py:115
  610.5 22.0 %copy-start.1 = (bf16[512,2048]{1,0:T(8,128)(2,1)S(1)}, bf16[512,2048]{1,0:T(8,128)(2,1)}, u32[]{:S(2)}) copy-start(bf16[512,2048]{1,0:T(8,128)(2,1)} %param.10) | copy-start | bytes 6291460
  620.5 11.1 %copy-start.10 = (f32[2048]{0:T(1024)S(1)}, f32[2048]{0:T(1024)}, u32[]{:S(2)}) copy-start(f32[2048]{0:T(1024)} %param.17) | copy-start | bytes 24580
  631.5 1.0 copy-start.4
Sparse Core Ops, SparseCore 0:
  11.6 27.5 reduce-scatter.2
  43.0 77.6 all-gather.1
  330.0 149.4 reduce-scatter.4
